TPU v7x, 512 devices: a whole 4x4x16 slice. The times are simulated.
512 devices in a mesh: expert: 8 (over y, core), mp: 64 (over x, z).
Axes of the slice: x: 4, y: 4, z: 16, core: 2. Of those that a mesh axis runs over, the one named last changes fastest.
Arguments:
- context: bfloat16 [4096, 2048], P('expert', 'mp'), may hold values from -6 to 6
- out_proj: bfloat16 [2048, 2048], P('mp'), may hold values from -1 to 1, as said below
- routes: int32 [4096, 2], P('expert'), may hold values from 0 to 7, all different within a row; in each aligned block of 512 rows (0 to 511, 512 to 1023, ...) at most 256 rows name the same one
- router_logits: float32 [4096, 2], P('expert'), may hold values from -8 to 8
- w_gate: bfloat16 [45056, 2048], P('mp', 'expert'), may hold values from -0.125 to 0.125
- w_up: bfloat16 [45056, 2048], P('mp', 'expert'), may hold values from -0.125 to 0.125
- w_down: bfloat16 [45056, 2048], P('mp', 'expert'), may hold values from -0.078125 to 0.078125
- norm_gain: float32 [2048], P('mp'), may hold values from 0.25 to 1.75
- request_order: int32 [4096], P('expert'), may hold values from 0 to 4095, each once
Outputs:
- restored: bfloat16 [4096, 2048], P('expert', 'mp')
Inputs may be any that keep to these rules, and one draw needn't show every extreme that they name: `routes`: each row names 2 different experts. Within each aligned block of 512 rows no expert is named by more than 256 rows, and in some blocks one expert is named by exactly 256 rows. `request_order`: A permutation of the 4096 token rows. `out_proj`: entries of the order of one over the square root of 2048.
All inputs are finite; a program needn't handle non-finite values.
Results may differ from a plain program's by a relative error of at most 0.0056.
Values may be sent and summed in bfloat16 or wider, within the bound.
No kernel may reach another device: no remote copies, remote signals or barrier semaphores. Data moves between devices by JAX's collectives and lax.ppermute only.
A program may use at most 64 MiB of HBM per device.

v0:
```python
import jax
import jax.numpy as jnp
from jax import lax
from jax.sharding import PartitionSpec as P

EXPERTS = 8
CAP = 256
epsilon = 1e-06


def slot_targets(routes, capacity, experts):
    flat_routes = routes.reshape(-1)
    onehot = (flat_routes[:, None] == jnp.arange(experts, dtype=jnp.int32)[None, :]).astype(
        jnp.int32
    )
    earlier = jnp.cumsum(onehot, axis=0) - onehot
    slot_index = jnp.sum(earlier * onehot, axis=1)
    return flat_routes * capacity + slot_index


def shards(
    context, out_proj, routes, router_logits, w_gate, w_up, w_down, norm_gain, request_order
):
    tok_rows = context.shape[0]
    feat_local = context.shape[1]
    model_width = out_proj.shape[1]
    mp_count = lax.axis_size("mp")
    copies = mp_count // EXPERTS
    capacity = CAP
    top_k = routes.shape[1]
    attended = jnp.einsum(
        "td,cd->tc",
        lax.all_gather(context, "mp", axis=1, tiled=True),
        out_proj,
        preferred_element_type=jnp.float32,
    ).astype(jnp.bfloat16)
    destination = slot_targets(routes, capacity, EXPERTS)
    source_rows = jnp.repeat(jnp.arange(tok_rows, dtype=jnp.int32), top_k)
    slotted = (
        jnp.zeros((EXPERTS * capacity, feat_local), jnp.bfloat16)
        .at[destination]
        .set(attended[source_rows])
    )
    slotted = jnp.repeat(slotted.reshape(EXPERTS, capacity, feat_local), copies, axis=0)
    outgoing = slotted.transpose(1, 0, 2).reshape(capacity, mp_count * feat_local)
    inbox_rows = lax.all_to_all(outgoing, "mp", split_axis=1, concat_axis=1, tiled=True)
    gate_next = jnp.einsum(
        "rd,hd->rh",
        inbox_rows,
        lax.all_gather(w_gate, "expert", axis=1, tiled=True),
        preferred_element_type=jnp.float32,
    )
    up_next = jnp.einsum(
        "rd,hd->rh",
        inbox_rows,
        lax.all_gather(w_up, "expert", axis=1, tiled=True),
        preferred_element_type=jnp.float32,
    )
    activated = (jax.nn.silu(gate_next) * up_next).astype(jnp.bfloat16)
    partial_value = jnp.dot(
        activated,
        lax.all_gather(w_down, "expert", axis=1, tiled=True),
        preferred_element_type=jnp.float32,
    )
    returned = lax.all_to_all(partial_value, "mp", split_axis=1, concat_axis=0, tiled=True)
    expert_out = jnp.sum(returned.reshape(EXPERTS, copies, capacity, feat_local), axis=1).reshape(
        EXPERTS * capacity, feat_local
    )
    picked = expert_out[destination].reshape(tok_rows, top_k, feat_local)
    weights = 1.0 / (1.0 + jnp.exp(router_logits[:, ::-1] - router_logits))
    branch = jnp.sum(picked * weights[:, :, None], axis=1)
    combined = attended.astype(jnp.float32) + branch
    squares = lax.psum(jnp.sum(combined * combined, axis=1), "mp")
    normed = (
        combined * norm_gain[None, :] * lax.rsqrt(squares / model_width + epsilon)[:, None]
    ).astype(jnp.bfloat16)
    everyone = lax.all_gather(normed, "expert", axis=0, tiled=True)
    return everyone[request_order]


def solution(mesh):
    placed = (
        P("expert", "mp"),
        P("mp", None),
        P("expert", None),
        P("expert", None),
        P("mp", "expert"),
        P("mp", "expert"),
        P("mp", "expert"),
        P("mp"),
        P("expert"),
    )
    return jax.shard_map(
        shards, mesh=mesh, in_specs=placed, out_specs=P("expert", "mp"), check_vma=False
    )
```

profile of v0, /device:TPU:1, one launch (start us, length us, event | category | flops | bytes accessed | tf_op | source)
XLA Modules:
  0.0 565.7 jit_solution(14208333560372502879)
XLA Ops:
  6.5 0.0 copy-start
  6.5 0.7 all-gather.5.cloned.1.call-update
  7.3 0.0 all-gather.7.cloned.1.call-start
  7.3 0.7 all-gather.7.cloned.1.call-update
  8.0 0.0 all-gather.11.cloned.1.call-start
  8.1 0.7 all-gather.11.cloned.1.call-update
  8.7 0.0 all-gather.9.cloned.1.call-start
  8.8 0.5 all-gather.9.cloned.1.call-update
  9.3 0.8 copy.42
  10.2 0.2 eq.29
  10.3 0.2 eq.25
  10.5 0.7 broadcast_multiply_fusion
  11.2 2.3 reduce-window.6
  13.5 0.3 slice_reduce_fusion
  13.7 0.2 reduce-window.9
  13.9 0.1 add_bitcast_fusion
  14.0 0.2 copy.41
  14.1 0.2 mul.55
  14.4 0.2 reshape.104
  14.6 133.1 %all-gather.5.cloned.1.call-done = bf16[512,2048]{0,1:T(8,128)(2,1)} async-done(((bf16[512,32]{0,1:T(8,128)(2,1)}), bf16[512,2048]{0,1:T(8,128)(2,1)}) %all-gather.5.cloned.1.call-update) | async-done | bytes 2097168 | tf_op jit(solution)/shard_map/all_gather | solution.py:33
  147.7 2.0 convolution_convert_fusion
  149.7 0.1 copy.44
  149.9 6.4 %scatter_custom_fusion = bf16[2048,32]{1,0:T(8,128)(2,1)S(1)} fusion(s32[1024]{0:T(1024)S(1)} %bitcast.48, bf16[512,32]{1,0:T(8,128)(2,1)S(1)} %copy.44, s32[1024]{0:T(1024)S(1)} %broadcast_clamp_fusion.1, bf16[]{:T(256)} %constant.10.clone.1), kind=kCustom, calls=%fused_computation.16 | custom fusion | bytes 131074 | tf_op jit(solution)/shard_map/scatter | solution.py:42
  156.3 0.2 copy.46
  156.5 1.2 broadcast_in_dim.10
  157.7 8.8 %all-to-all-start = ((bf16[256,64,32]{0,2,1:T(8,128)(2,1)}), bf16[256,64,32]{0,2,1:T(8,128)(2,1)S(1)}, u32[]{:S(2)}, u32[]{:S(2)}) async-start(bf16[256,64,32]{0,2,1:T(8,128)(2,1)} %bitcast.6), calls=%async_computation | async-start | bytes 2097152 | tf_op jit(solution)/shard_map/all_to_all | solution.py:46
  166.5 26.9 %all-gather.7.cloned.1.call-done = bf16[704,2048]{1,0:T(8,128)(2,1)} async-done(((bf16[704,256]{1,0:T(8,128)(2,1)}), bf16[704,2048]{1,0:T(8,128)(2,1)}) %all-gather.7.cloned.1.call-update) | async-done | bytes 2883600 | tf_op jit(solution)/shard_map/all_gather | solution.py:50
  193.4 12.3 %all-to-all-done = bf16[256,64,32]{0,2,1:T(8,128)(2,1)S(1)} async-done(((bf16[256,64,32]{0,2,1:T(8,128)(2,1)}), bf16[256,64,32]{0,2,1:T(8,128)(2,1)S(1)}, u32[]{:S(2)}, u32[]{:S(2)}) %all-to-all-start) | async-done | bytes 1048608 | tf_op jit(solution)/shard_map/all_to_all | solution.py:46
  205.6 2.7 fusion.16
  208.4 26.4 %all-gather.11.cloned.1.call-done = bf16[704,2048]{1,0:T(8,128)(2,1)} async-done(((bf16[704,256]{1,0:T(8,128)(2,1)}), bf16[704,2048]{1,0:T(8,128)(2,1)}) %all-gather.11.cloned.1.call-update) | async-done | bytes 2883600 | tf_op jit(solution)/shard_map/all_gather | solution.py:62
  234.8 41.3 %all-gather.9.cloned.1.call-done = bf16[704,2048]{1,0:T(8,128)(2,1)} async-done(((bf16[704,256]{1,0:T(8,128)(2,1)}), bf16[704,2048]{1,0:T(8,128)(2,1)}) %all-gather.9.cloned.1.call-update) | async-done | bytes 2883600 | tf_op jit(solution)/shard_map/all_gather | solution.py:56
  276.1 7.2 %fusion.1 = f32[256,2048]{0,1:T(8,128)} fusion(bf16[704,2048]{1,0:T(8,128)(2,1)} %all-gather.11.cloned.1.call-done, bf16[704,2048]{1,0:T(8,128)(2,1)} %all-gather.9.cloned.1.call-done, bf16[256,2048]{0,1:T(8,128)(2,1)S(1)} %bitcast.46, f32[256,704]{0,1:T(8,128)S(1)} %fusion.16), kind=kOutput, calls=%fused_computation.8 | convolution fusion | flops 1477476352 | bytes 9633792 | tf_op jit(solution)/shard_map/dot_general | solution.py:60
  283.4 15.6 %all-to-all-start.1 = ((f32[256,64,32]{0,2,1:T(8,128)}), f32[256,64,32]{0,2,1:T(8,128)S(1)}, u32[]{:S(2)}, u32[]{:S(2)}) async-start(f32[256,64,32]{0,2,1:T(8,128)} %bitcast.43), calls=%async_computation.1 | async-start | bytes 4194304 | tf_op jit(solution)/shard_map/all_to_all | solution.py:65
  299.0 0.1 rev.3
  299.2 0.1 copy.49
  299.4 91.4 %all-to-all-done.1 = f32[256,64,32]{0,2,1:T(8,128)S(1)} async-done(((f32[256,64,32]{0,2,1:T(8,128)}), f32[256,64,32]{0,2,1:T(8,128)S(1)}, u32[]{:S(2)}, u32[]{:S(2)}) %all-to-all-start.1) | async-done | bytes 2097184 | tf_op jit(solution)/shard_map/all_to_all | solution.py:65
  390.8 0.2 bitcast_reduce_fusion
  390.9 0.3 copy.48
  391.3 0.0 copy-start.3
  391.3 2.8 gather_fusion
  394.1 2.8 multiply_reduce_fusion
  396.9 0.1 copy.50
  397.1 118.5 %psum.7 = f32[512]{0:T(512)S(1)} all-reduce(f32[512]{0:T(512)S(1)} %multiply_reduce_fusion.1), channel_id=1, replica_groups=mesh['expert'=8,'mp'=64] {'mp'}, use_global_device_ids=true, to_apply=%region_7.8 | all-reduce | flops 512 | bytes 4096 | tf_op jit(solution)/shard_map/psum | solution.py:73
  515.6 0.1 multiply_convert_fusion
  515.6 41.0 %all_gather.19 = bf16[4096,32]{0,1:T(8,128)(2,1)S(1)} all-gather(bf16[512,32]{0,1:T(8,128)(2,1)S(1)} %multiply_convert_fusion), channel_id=1, replica_groups=mesh['expert'=8,'mp'=64] {'expert'}, dimensions={0}, use_global_device_ids=true | all-gather | bytes 294912 | tf_op jit(solution)/shard_map/all_gather | solution.py:77
  556.6 0.5 copy.51
  557.1 1.3 gather_fusion.1
  558.4 0.7 copy.52
  (19 shorter events, 0.2 us)
Async XLA Ops:
  6.5 141.2 %copy-start = (bf16[32,2048]{1,0:T(8,128)(2,1)S(1)}, bf16[32,2048]{1,0:T(8,128)(2,1)}, u32[]{:S(2)}) copy-start(bf16[32,2048]{1,0:T(8,128)(2,1)} %param.10) | copy-start | bytes 393220
  6.5 141.2 %all-gather.5.cloned.1.call-start = ((), (), s32[]{:S(2)}) async-start(), calls=%async_computation.2 | async-start | bytes 2129920 | tf_op jit(solution)/shard_map/all_gather | solution.py:33
  7.3 186.1 %all-gather.7.cloned.1.call-start = ((), (), s32[]{:S(2)}) async-start(), calls=%async_computation.3 | async-start | bytes 3244032 | tf_op jit(solution)/shard_map/all_gather | solution.py:50
  8.0 226.8 %all-gather.11.cloned.1.call-start = ((), (), s32[]{:S(2)}) async-start(), calls=%async_computation.5 | async-start | bytes 3244032 | tf_op jit(solution)/shard_map/all_gather | solution.py:62
  8.7 267.4 %all-gather.9.cloned.1.call-start = ((), (), s32[]{:S(2)}) async-start(), calls=%async_computation.4 | async-start | bytes 3244032 | tf_op jit(solution)/shard_map/all_gather | solution.py:56
  157.7 48.0 %all-to-all-start = ((bf16[256,64,32]{0,2,1:T(8,128)(2,1)}), bf16[256,64,32]{0,2,1:T(8,128)(2,1)S(1)}, u32[]{:S(2)}, u32[]{:S(2)}) async-start(bf16[256,64,32]{0,2,1:T(8,128)(2,1)} %bitcast.6), calls=%async_computation | async-start | bytes 2097152 | tf_op jit(solution)/shard_map/all_to_all | solution.py:46
  283.4 15.7 %copy-start.1 = (f32[512,2]{0,1:T(2,128)S(1)}, f32[512,2]{0,1:T(2,128)}, u32[]{:S(2)}) copy-start(f32[512,2]{0,1:T(2,128)} %param.12) | copy-start | bytes 12292
  283.4 16.0 %copy-start.2 = (s32[512]{0:T(512)S(1)}, s32[512]{0:T(512)}, u32[]{:S(2)}) copy-start(s32[512]{0:T(512)} %param.17) | copy-start | bytes 6148
  283.4 107.4 %all-to-all-start.1 = ((f32[256,64,32]{0,2,1:T(8,128)}), f32[256,64,32]{0,2,1:T(8,128)S(1)}, u32[]{:S(2)}, u32[]{:S(2)}) async-start(f32[256,64,32]{0,2,1:T(8,128)} %bitcast.43), calls=%async_computation.1 | async-start | bytes 4194304 | tf_op jit(solution)/shard_map/all_to_all | solution.py:65
  391.3 124.3 %copy-start.3 = (f32[32]{0:T(128)S(1)}, f32[32]{0:T(128)}, u32[]{:S(2)}) copy-start(f32[32]{0:T(128)} %param.16) | copy-start | bytes 388
Sparse Core Ops, SparseCore 0:
  10.3 137.3 all-gather.4
  149.8 43.5 all-gather.6
  195.5 39.2 all-gather.10
  236.8 39.2 all-gather.8
where the time goes:
time: 566 us
  waiting for transfers between devices  334 us (59%)
  blocking collectives  159 us (28%)
  starting transfers between devices  24.5 us (4%)
  local copies, waits for them, and re-layouts  16 us (3%)
  between operations  13.4 us (2%)
  matrix products  12 us (2%)
  other arithmetic  6.35 us (1%)
    all_gather x1, waiting for transfers between devices, shards(): lax.all_gather(context, 'mp', axis=1, tiled=True)  133 us
    psum x1, blocking collectives, shards(): squares = lax.psum(jnp.sum(combined * combined, axis=1), 'mp')  118 us
    all_to_all x1, waiting for transfers between devices, shards(): lax.all_to_all(partial_value, 'mp', split_axis=1, concat_axis=0, tiled=True)  91.4 us
    all_gather x1, waiting for transfers between devices, shards(): lax.all_gather(w_up, 'expert', axis=1, tiled=True)  41.3 us
    all_gather x1, blocking collectives, shards(): everyone = lax.all_gather(normed, 'expert', axis=0, tiled=True)  41 us
    all_gather x1, waiting for transfers between devices, shards(): lax.all_gather(w_gate, 'expert', axis=1, tiled=True)  26.9 us
    all_gather x1, waiting for transfers between devices, shards(): lax.all_gather(w_down, 'expert', axis=1, tiled=True)  26.4 us
    all_to_all x1, starting transfers between devices, shards(): lax.all_to_all(partial_value, 'mp', split_axis=1, concat_axis=0, tiled=True)  15.6 us
  transfers between devices with their start and end apart: 6, of which 6 were waited for; matrix products, arithmetic and copies ran while one was open for 3% of the time, Pallas kernels for 0%

commit v1 on v0

--- a/solution.py
+++ b/solution.py
@@ -74,7 +74,14 @@
     normed = (
         combined * norm_gain[None, :] * lax.rsqrt(squares / model_width + epsilon)[:, None]
     ).astype(jnp.bfloat16)
-    everyone = lax.all_gather(normed, "expert", axis=0, tiled=True)
+    ring = [normed]
+    for hop in range(7):
+        ring.append(lax.ppermute(ring[-1], "expert", [(dev, (dev + 1) % 8) for dev in range(8)]))
+    everyone = jnp.roll(
+        jnp.concatenate(ring[::-1], axis=0),
+        (lax.axis_index("expert") + 1) * ring[0].shape[0],
+        axis=0,
+    )
     return everyone[request_order]
 
 

time: 566 us -> 582 us (1.028)
  blocking collectives: 159 us -> 118 us
  starting transfers between devices: 24.5 us -> 58.7 us
  waiting for transfers between devices: 334 us -> 356 us
    all_gather x1 -> x0, blocking collectives: 41 us -> none  [shards(): everyone = lax.all_gather(normed, 'expert', axis=0, tiled=True)]
    ppermute x0 -> x7, starting transfers between devices: none -> 34.2 us  [shards(): lax.ppermute(ring[-1], 'expert', [(dev, (dev + 1) % 8) for dev in range(8)])]
    ppermute x0 -> x7, waiting for transfers between devices: none -> 22.1 us  [shards(): lax.ppermute(ring[-1], 'expert', [(dev, (dev + 1) % 8) for dev in range(8)])]
  transfers between devices with their start and end apart: 6 -> 13, of which waited for: 6 -> 13; matrix products, arithmetic and copies ran while one was open for 3% -> 3% of each run, Pallas kernels for 0% -> 0%
where the time goes in v1:
time: 582 us; the launch traced here: 581 us
  waiting for transfers between devices  356 us (61%)
  blocking collectives  118 us (20%)
  starting transfers between devices  58.7 us (10%)
  local copies, waits for them, and re-layouts  16.1 us (3%)
  between operations  13.5 us (2%)
  matrix products  12 us (2%)
  other arithmetic  6.35 us (1%)
    all_gather x1, waiting for transfers between devices, shards(): lax.all_gather(context, 'mp', axis=1, tiled=True)  133 us
    psum x1, blocking collectives, shards(): squares = lax.psum(jnp.sum(combined * combined, axis=1), 'mp')  118 us
    all_to_all x1, waiting for transfers between devices, shards(): lax.all_to_all(partial_value, 'mp', split_axis=1, concat_axis=0, tiled=True)  91.4 us
    all_gather x1, waiting for transfers between devices, shards(): lax.all_gather(w_up, 'expert', axis=1, tiled=True)  41.3 us
    ppermute x7, starting transfers between devices, shards(): lax.ppermute(ring[-1], 'expert', [(dev, (dev + 1) % 8) for dev in range(8)])  34.2 us
    all_gather x1, waiting for transfers between devices, shards(): lax.all_gather(w_gate, 'expert', axis=1, tiled=True)  26.9 us
    all_gather x1, waiting for transfers between devices, shards(): lax.all_gather(w_down, 'expert', axis=1, tiled=True)  26.5 us
    ppermute x7, waiting for transfers between devices, shards(): lax.ppermute(ring[-1], 'expert', [(dev, (dev + 1) % 8) for dev in range(8)])  22.1 us
  transfers between devices with their start and end apart: 13, of which 13 were waited for; matrix products, arithmetic and copies ran while one was open for 3% of the time, Pallas kernels for 0%

profile of v1, /device:TPU:1, one launch (start us, length us, event | category | flops | bytes accessed | tf_op | source)
XLA Modules:
  0.0 581.2 jit_solution(9365201621051801385)
XLA Ops:
  6.5 0.7 all-gather.5.cloned.1.call-update
  7.3 0.7 all-gather.7.cloned.1.call-update
  8.1 0.7 all-gather.11.cloned.1.call-update
  8.8 0.5 all-gather.9.cloned.1.call-update
  9.3 0.8 copy.42
  10.2 0.2 eq.32
  10.3 0.2 eq.28
  10.5 0.7 broadcast_multiply_fusion
  11.2 2.3 reduce-window.6
  13.5 0.3 slice_reduce_fusion
  13.7 0.2 reduce-window.9
  14.0 0.2 copy.41
  14.1 0.2 mul.58
  14.4 0.2 reshape.104
  14.6 133.1 %all-gather.5.cloned.1.call-done = bf16[512,2048]{0,1:T(8,128)(2,1)} async-done(((bf16[512,32]{0,1:T(8,128)(2,1)}), bf16[512,2048]{0,1:T(8,128)(2,1)}) %all-gather.5.cloned.1.call-update) | async-done | bytes 2097168 | tf_op jit(solution)/shard_map/all_gather | solution.py:33
  147.7 2.0 convolution_convert_fusion
  149.9 6.4 %scatter_custom_fusion = bf16[2048,32]{1,0:T(8,128)(2,1)S(1)} fusion(s32[1024]{0:T(1024)S(1)} %bitcast.47, bf16[512,32]{1,0:T(8,128)(2,1)S(1)} %copy.44, s32[1024]{0:T(1024)S(1)} %broadcast_clamp_fusion.1, bf16[]{:T(256)} %constant.22.clone.1), kind=kCustom, calls=%fused_computation.16 | custom fusion | bytes 131074 | tf_op jit(solution)/shard_map/scatter | solution.py:42
  156.3 0.2 copy.46
  156.5 1.2 broadcast_in_dim.10
  157.7 8.8 %all-to-all-start = ((bf16[256,64,32]{0,2,1:T(8,128)(2,1)}), bf16[256,64,32]{0,2,1:T(8,128)(2,1)S(1)}, u32[]{:S(2)}, u32[]{:S(2)}) async-start(bf16[256,64,32]{0,2,1:T(8,128)(2,1)} %bitcast.6), calls=%async_computation | async-start | bytes 2097152 | tf_op jit(solution)/shard_map/all_to_all | solution.py:46
  166.5 26.9 %all-gather.7.cloned.1.call-done = bf16[704,2048]{1,0:T(8,128)(2,1)} async-done(((bf16[704,256]{1,0:T(8,128)(2,1)}), bf16[704,2048]{1,0:T(8,128)(2,1)}) %all-gather.7.cloned.1.call-update) | async-done | bytes 2883600 | tf_op jit(solution)/shard_map/all_gather | solution.py:50
  193.4 12.2 %all-to-all-done = bf16[256,64,32]{0,2,1:T(8,128)(2,1)S(1)} async-done(((bf16[256,64,32]{0,2,1:T(8,128)(2,1)}), bf16[256,64,32]{0,2,1:T(8,128)(2,1)S(1)}, u32[]{:S(2)}, u32[]{:S(2)}) %all-to-all-start) | async-done | bytes 1048608 | tf_op jit(solution)/shard_map/all_to_all | solution.py:46
  205.6 2.7 fusion.16
  208.4 26.5 %all-gather.11.cloned.1.call-done = bf16[704,2048]{1,0:T(8,128)(2,1)} async-done(((bf16[704,256]{1,0:T(8,128)(2,1)}), bf16[704,2048]{1,0:T(8,128)(2,1)}) %all-gather.11.cloned.1.call-update) | async-done | bytes 2883600 | tf_op jit(solution)/shard_map/all_gather | solution.py:62
  234.8 41.3 %all-gather.9.cloned.1.call-done = bf16[704,2048]{1,0:T(8,128)(2,1)} async-done(((bf16[704,256]{1,0:T(8,128)(2,1)}), bf16[704,2048]{1,0:T(8,128)(2,1)}) %all-gather.9.cloned.1.call-update) | async-done | bytes 2883600 | tf_op jit(solution)/shard_map/all_gather | solution.py:56
  276.1 7.2 %fusion.1 = f32[256,2048]{0,1:T(8,128)} fusion(bf16[704,2048]{1,0:T(8,128)(2,1)} %all-gather.11.cloned.1.call-done, bf16[704,2048]{1,0:T(8,128)(2,1)} %all-gather.9.cloned.1.call-done, bf16[256,2048]{0,1:T(8,128)(2,1)S(1)} %bitcast.46, f32[256,704]{0,1:T(8,128)S(1)} %fusion.16), kind=kOutput, calls=%fused_computation.8 | convolution fusion | flops 1477476352 | bytes 9633792 | tf_op jit(solution)/shard_map/dot_general | solution.py:60
  283.4 15.6 %all-to-all-start.1 = ((f32[256,64,32]{0,2,1:T(8,128)}), f32[256,64,32]{0,2,1:T(8,128)S(1)}, u32[]{:S(2)}, u32[]{:S(2)}) async-start(f32[256,64,32]{0,2,1:T(8,128)} %bitcast.43), calls=%async_computation.1 | async-start | bytes 4194304 | tf_op jit(solution)/shard_map/all_to_all | solution.py:65
  299.2 0.1 copy.49
  299.4 91.4 %all-to-all-done.1 = f32[256,64,32]{0,2,1:T(8,128)S(1)} async-done(((f32[256,64,32]{0,2,1:T(8,128)}), f32[256,64,32]{0,2,1:T(8,128)S(1)}, u32[]{:S(2)}, u32[]{:S(2)}) %all-to-all-start.1) | async-done | bytes 2097184 | tf_op jit(solution)/shard_map/all_to_all | solution.py:65
  390.8 0.2 bitcast_reduce_fusion
  391.0 0.3 copy.48
  391.3 2.8 gather_fusion
  394.1 2.8 multiply_reduce_fusion
  397.1 118.5 %psum.7 = f32[512]{0:T(512)S(1)} all-reduce(f32[512]{0:T(512)S(1)} %multiply_reduce_fusion.1), channel_id=1, replica_groups=mesh['expert'=8,'mp'=64] {'mp'}, use_global_device_ids=true, to_apply=%region_7.8 | all-reduce | flops 512 | bytes 4096 | tf_op jit(solution)/shard_map/psum | solution.py:73
  515.6 28.9 %collective-permute-start = (bf16[512,32]{0,1:T(8,128)(2,1)S(1)}, bf16[512,32]{0,1:T(8,128)(2,1)S(1)}, u32[]{:S(2)}, u32[]{:S(2)}) collective-permute-start(bf16[512,32]{0,1:T(8,128)(2,1)S(1)} %multiply_convert_fusion), channel_id=1, source_target_pairs={{0,64},{64,128},{128,192},{192,256},{256,320},{320,384},{384,448},... | collective-permute-start | bytes 98312 | tf_op jit(solution)/shard_map/ppermute | solution.py:79
  544.6 1.0 collective-permute-done
  545.6 2.3 collective-permute-start.1
  547.9 1.3 collective-permute-done.1
  549.2 2.1 collective-permute-start.2
  551.2 2.5 collective-permute-done.2
  553.7 0.9 collective-permute-start.3
  554.6 3.7 collective-permute-done.3
  558.3 4.5 collective-permute-done.4
  562.8 4.5 collective-permute-done.5
  567.4 4.5 collective-permute-done.6
  572.1 0.5 copy.51
  572.7 1.3 gather_fusion.1
  574.0 0.7 copy.52
  (48 shorter events, 0.9 us)
Async XLA Ops:
  6.5 141.2 %copy-start = (bf16[32,2048]{1,0:T(8,128)(2,1)S(1)}, bf16[32,2048]{1,0:T(8,128)(2,1)}, u32[]{:S(2)}) copy-start(bf16[32,2048]{1,0:T(8,128)(2,1)} %param.10) | copy-start | bytes 393220
  6.5 141.2 %all-gather.5.cloned.1.call-start = ((), (), s32[]{:S(2)}) async-start(), calls=%async_computation.2 | async-start | bytes 2129920 | tf_op jit(solution)/shard_map/all_gather | solution.py:33
  7.3 186.1 %all-gather.7.cloned.1.call-start = ((), (), s32[]{:S(2)}) async-start(), calls=%async_computation.3 | async-start | bytes 3244032 | tf_op jit(solution)/shard_map/all_gather | solution.py:50
  8.0 226.8 %all-gather.11.cloned.1.call-start = ((), (), s32[]{:S(2)}) async-start(), calls=%async_computation.5 | async-start | bytes 3244032 | tf_op jit(solution)/shard_map/all_gather | solution.py:62
  8.7 267.4 %all-gather.9.cloned.1.call-start = ((), (), s32[]{:S(2)}) async-start(), calls=%async_computation.4 | async-start | bytes 3244032 | tf_op jit(solution)/shard_map/all_gather | solution.py:56
  157.7 48.0 %all-to-all-start = ((bf16[256,64,32]{0,2,1:T(8,128)(2,1)}), bf16[256,64,32]{0,2,1:T(8,128)(2,1)S(1)}, u32[]{:S(2)}, u32[]{:S(2)}) async-start(bf16[256,64,32]{0,2,1:T(8,128)(2,1)} %bitcast.6), calls=%async_computation | async-start | bytes 2097152 | tf_op jit(solution)/shard_map/all_to_all | solution.py:46
  283.4 15.7 %copy-start.1 = (f32[512,2]{0,1:T(2,128)S(1)}, f32[512,2]{0,1:T(2,128)}, u32[]{:S(2)}) copy-start(f32[512,2]{0,1:T(2,128)} %param.12) | copy-start | bytes 12292
  283.4 16.0 %copy-start.2 = (s32[512]{0:T(512)S(1)}, s32[512]{0:T(512)}, u32[]{:S(2)}) copy-start(s32[512]{0:T(512)} %param.17) | copy-start | bytes 6148
  283.4 107.4 %all-to-all-start.1 = ((f32[256,64,32]{0,2,1:T(8,128)}), f32[256,64,32]{0,2,1:T(8,128)S(1)}, u32[]{:S(2)}, u32[]{:S(2)}) async-start(f32[256,64,32]{0,2,1:T(8,128)} %bitcast.43), calls=%async_computation.1 | async-start | bytes 4194304 | tf_op jit(solution)/shard_map/all_to_all | solution.py:65
  391.3 124.3 %copy-start.3 = (f32[32]{0:T(128)S(1)}, f32[32]{0:T(128)}, u32[]{:S(2)}) copy-start(f32[32]{0:T(128)} %param.16) | copy-start | bytes 388
  515.6 30.0 %collective-permute-start = (bf16[512,32]{0,1:T(8,128)(2,1)S(1)}, bf16[512,32]{0,1:T(8,128)(2,1)S(1)}, u32[]{:S(2)}, u32[]{:S(2)}) collective-permute-start(bf16[512,32]{0,1:T(8,128)(2,1)S(1)} %multiply_convert_fusion), channel_id=1, source_target_pairs={{0,64},{64,128},{128,192},{192,256},{256,320},{320,384},{384,448},... | collective-permute-start | bytes 98312 | tf_op jit(solution)/shard_map/ppermute | solution.py:79
  545.6 3.6 collective-permute-start.1
  549.2 4.6 collective-permute-start.2
  553.7 4.6 collective-permute-start.3
  558.3 4.6 collective-permute-start.4
  562.8 4.6 collective-permute-start.5
  567.4 4.6 collective-permute-start.6
Sparse Core Ops, SparseCore 0:
  10.3 137.3 all-gather.4
  149.8 43.5 all-gather.6
  195.5 39.2 all-gather.10
  236.8 39.2 all-gather.8
